TPU v7x, 256 devices: a whole 4x4x8 slice. The times are simulated.
256 devices in a mesh: dp: 4 (over x), expert: 64 (over z, y, core).
Axes of the slice: x: 4, y: 4, z: 8, core: 2. Of those that a mesh axis runs over, the one named last changes fastest.
Arguments:
- tokens: bfloat16 [4096, 2048], P(('dp', 'expert')), may hold values from -6 to 6
- expert_ids: int32 [4096, 8], P(('dp', 'expert')), may hold values from 0 to 127, all different within a row; in each aligned block of 16 rows (0 to 15, 16 to 31, ...) at most 2 rows name the same one
- gate_weights: float32 [4096, 8], P(('dp', 'expert')), may hold values from 0.1 to 1
- hot_experts: int32 [2], replicated, may hold values from 0 to 127, as said below
- capacity: int32 [128], replicated, may hold values from 32 to 64
- w_in: bfloat16 [128, 2048, 1536], P('expert', None, 'dp'), may hold values from -0.125 to 0.125
- w_out: bfloat16 [128, 1536, 2048], P('expert', 'dp'), may hold values from -0.15625 to 0.15625
- grad_y: bfloat16 [4096, 2048], P(('dp', 'expert')), may hold values from -1.5 to 1.5
Outputs:
- mixed: bfloat16 [4096, 2048], P(('dp', 'expert'))
- token_grad: bfloat16 [4096, 2048], P(('dp', 'expert'))
- gate_grad: float32 [4096, 8], P(('dp', 'expert'))
- grad_w_in: bfloat16 [128, 2048, 1536], P('expert', None, 'dp')
- grad_w_out: bfloat16 [128, 1536, 2048], P('expert', 'dp')
Inputs may be any that keep to these rules, and one draw needn't show every extreme that they name: `expert_ids`: among the tokens of one device no expert is named more than 2 times, a bound that some block reaches. `hot_experts`: 2 different experts; the last entry is always expert 128 - 1.
All inputs are finite; a program needn't handle non-finite values.
Results may differ from a plain program's by a relative error of at most 0.012.
Values may be sent and summed in bfloat16 or wider, within the bound.
No kernel may reach another device: no remote copies, remote signals or barrier semaphores. Data moves between devices by JAX's collectives and lax.ppermute only.
A program may use at most 128 MiB of HBM per device.

v0:
```python
import jax
import jax.numpy as jnp
from jax import lax
from jax.sharding import PartitionSpec as P


def prefix(part, axis, combine, identity):
    place = lax.axis_index(axis)
    gathered = lax.all_gather(part, axis)
    state = jnp.zeros_like(part) + jnp.asarray(identity, part.dtype)

    def one(turn, state):
        return combine(state, lax.dynamic_index_in_dim(gathered, turn, 0, False))

    return lax.fori_loop(0, place, one, state)


def silu_terms(pre_act):
    sig_val = jax.nn.sigmoid(pre_act)
    return (pre_act * sig_val, sig_val * (1.0 + pre_act * (1.0 - sig_val)))


def expert_math(rows_x, rows_g, weight_in, weight_out):
    pre_act = jnp.einsum("gerd,edh->gerh", rows_x, weight_in, preferred_element_type=jnp.float32)
    act_full, slope_val = silu_terms(pre_act)
    act_low = act_full.astype(jnp.bfloat16)
    out_part = jnp.einsum("gerh,ehd->gerd", act_low, weight_out, preferred_element_type=jnp.float32)
    back_act = jnp.einsum("gerd,ehd->gerh", rows_g, weight_out, preferred_element_type=jnp.float32)
    pre_grad = (back_act * slope_val).astype(jnp.bfloat16)
    in_part = jnp.einsum("gerh,edh->gerd", pre_grad, weight_in, preferred_element_type=jnp.float32)
    grad_in = jnp.einsum("gerd,gerh->edh", rows_x, pre_grad, preferred_element_type=jnp.float32)
    grad_out = jnp.einsum("gerh,gerd->ehd", act_low, rows_g, preferred_element_type=jnp.float32)
    stacked = jnp.stack([out_part, in_part], axis=1)
    partial_terms = lax.optimization_barrier(stacked.astype(jnp.bfloat16)).astype(jnp.float32)
    return (partial_terms, grad_in, grad_out)


def local(tokens, expert_ids, gate_weights, hot_experts, capacity, w_in, w_out, grad_y):
    highest = lax.Precision.HIGHEST
    expert_devs = lax.axis_size("expert")
    tok_rows, top_k = expert_ids.shape
    local_experts = w_in.shape[0]
    expert_total = local_experts * expert_devs
    slot_count = max(2, 3 * tok_rows * top_k // (2 * expert_total))
    feature_dim = tokens.shape[1]
    labels = jnp.arange(expert_total, dtype=jnp.int32)
    name_hit = (expert_ids[:, :, None] == labels).astype(jnp.int32)
    per_token = jnp.sum(name_hit, axis=1)
    local_counts = jnp.sum(per_token, axis=0)
    earlier = prefix(
        local_counts, "expert", lambda first, second: first + second, jnp.zeros_like(local_counts)
    )
    within_dev = jnp.cumsum(per_token, axis=0) - per_token
    rank_of = earlier[None, :] + within_dev
    is_hot = jnp.any(labels[:, None] == hot_experts[None, :], axis=1)
    keep_mask = jnp.logical_or(is_hot[None, :], rank_of < capacity[None, :]).astype(jnp.float32)
    slot_hit = (within_dev[:, :, None] == jnp.arange(slot_count, dtype=jnp.int32)).astype(
        jnp.float32
    )
    chosen = name_hit.astype(jnp.float32) * keep_mask[:, None, :]
    pick_mask = chosen[:, :, :, None] * slot_hit[:, None, :, :]
    sending = jnp.ones((expert_total,), jnp.float32)
    send_picks = pick_mask * sending[None, None, :, None]
    rows_sel = jnp.sum(send_picks, axis=1)
    gate_sel = jnp.einsum("tkes,tk->tes", send_picks, gate_weights, precision=highest)
    grad_f32 = grad_y.astype(jnp.float32)
    x_buf = jnp.einsum(
        "tes,td->esd", rows_sel.astype(jnp.bfloat16), tokens, preferred_element_type=jnp.float32
    ).astype(jnp.bfloat16)
    x_buf = x_buf.reshape(expert_devs, local_experts, slot_count, feature_dim)
    g_buf = jnp.einsum("tes,td->esd", gate_sel, grad_f32, precision=highest).astype(jnp.bfloat16)
    g_buf = g_buf.reshape(expert_devs, local_experts, slot_count, feature_dim)
    x_recv, g_recv = (
        lax.all_to_all(x_buf, "expert", split_axis=0, concat_axis=2, tiled=True),
        lax.all_to_all(g_buf, "expert", split_axis=0, concat_axis=2, tiled=True),
    )
    xg_all, gg_all = (
        lax.all_gather(x_recv, "dp", axis=0, tiled=True),
        lax.all_gather(g_recv, "dp", axis=0, tiled=True),
    )
    partial_terms, grad_wi, grad_wo = expert_math(xg_all, gg_all, w_in, w_out)
    summed = lax.psum_scatter(
        partial_terms.astype(jnp.bfloat16), "dp", scatter_dimension=0, tiled=True
    ).astype(jnp.float32)
    out_rows = summed[:, 0].astype(jnp.bfloat16)
    in_rows = summed[:, 1].astype(jnp.bfloat16)
    out_back, in_back = (
        lax.all_to_all(out_rows, "expert", split_axis=2, concat_axis=0, tiled=True),
        lax.all_to_all(in_rows, "expert", split_axis=2, concat_axis=0, tiled=True),
    )
    out_f32 = out_back.reshape(expert_total, slot_count, feature_dim).astype(jnp.float32)
    in_f32 = in_back.reshape(expert_total, slot_count, feature_dim).astype(jnp.float32)
    mixed = jnp.einsum("tes,esd->td", gate_sel, out_f32, precision=highest)
    token_grad = jnp.einsum("tes,esd->td", rows_sel, in_f32, precision=highest)
    dot_vals = jnp.einsum("td,esd->tes", grad_f32, out_f32, precision=highest)
    gate_grad = jnp.einsum("tkes,tes->tk", send_picks, dot_vals, precision=highest)
    return (
        mixed.astype(jnp.bfloat16),
        token_grad.astype(jnp.bfloat16),
        gate_grad,
        grad_wi.astype(jnp.bfloat16),
        grad_wo.astype(jnp.bfloat16),
    )


def solution(mesh):
    in_specs = (
        P(("dp", "expert"), None),
        P(("dp", "expert"), None),
        P(("dp", "expert"), None),
        P(),
        P(),
        P("expert", None, "dp"),
        P("expert", "dp", None),
        P(("dp", "expert"), None),
    )
    out_specs = (
        P(("dp", "expert"), None),
        P(("dp", "expert"), None),
        P(("dp", "expert"), None),
        P("expert", None, "dp"),
        P("expert", "dp", None),
    )
    return jax.shard_map(local, mesh=mesh, in_specs=in_specs, out_specs=out_specs, check_vma=False)
```

profile of v0, /device:TPU:1, one launch (start us, length us, event | category | flops | bytes accessed | tf_op | source)
XLA Modules:
  0.0 473.5 jit_solution(17353640763029097142)
XLA Ops:
  9.0 44.3 %all-gather.1 = s32[64,1,128]{2,1,0:T(1,128)S(1)} all-gather(s32[1,1,128]{2,1,0:T(1,128)S(1)} %bitcast.146), channel_id=2, replica_groups=mesh['dp'=4,'expert'=64] {'expert'}, dimensions={0}, use_global_device_ids=true | all-gather | bytes 33280 | tf_op jit(solution)/shard_map/all_gather | solution.py:9
  56.4 2.5 reshape.109
  59.0 2.4 copy.33
  61.4 35.9 %all_to_all.66 = bf16[64,2,2,2048]{3,1,2,0:T(2,128)(2,1)S(1)} all-to-all(bf16[64,2,2,2048]{3,1,2,0:T(2,128)(2,1)S(1)} %copy.33), channel_id=1, replica_groups=mesh['dp'=4,'expert'=64] {'expert'}, dimensions={0} | all-to-all | bytes 2097152 | tf_op jit(solution)/shard_map/all_to_all | solution.py:74
  101.1 2.5 reshape.110
  103.6 2.4 copy.35
  106.0 34.2 %all_to_all.67 = bf16[64,2,2,2048]{3,1,2,0:T(2,128)(2,1)S(1)} all-to-all(bf16[64,2,2,2048]{3,1,2,0:T(2,128)(2,1)S(1)} %copy.35), channel_id=1, replica_groups=mesh['dp'=4,'expert'=64] {'expert'}, dimensions={0} | all-to-all | bytes 2097152 | tf_op jit(solution)/shard_map/all_to_all | solution.py:75
  141.8 4.5 all-gather.5.cloned.1.call-done
  146.3 5.5 %fusion.1 = f32[2,4,128,384]{3,2,1,0:T(8,128)S(1)} fusion(bf16[4,2,128,2048]{3,2,0,1:T(8,128)(2,1)} %all-gather.5.cloned.1.call-done, bf16[2,2048,384]{2,1,0:T(8,128)(2,1)} %param.15), kind=kOutput, calls=%fused_computation.7 | convolution fusion | flops 1610612736 | bytes 8912896 | tf_op jit(solution)/shard_map/gerd,edh->gerh/dot_general | solution.py:24
  153.0 4.3 convert_bitcast_fusion.1
  157.3 42.5 %all-gather.7.cloned.1.call-done = bf16[4,2,128,2048]{3,2,0,1:T(8,128)(2,1)} async-done(((bf16[1,2,128,2048]{3,2,0,1:T(8,128)(2,1)}), bf16[4,2,128,2048]{3,2,0,1:T(8,128)(2,1)}) %all-gather.7.cloned.1.call-update) | async-done | bytes 4194320 | tf_op jit(solution)/shard_map/all_gather | solution.py:79
  199.8 5.2 %fusion.8 = bf16[4,2,128,384]{3,2,0,1:T(8,128)(2,1)S(1)} fusion(f32[2,4,128,384]{3,2,1,0:T(8,128)} %copy-done.9, bf16[4,2,128,2048]{3,2,0,1:T(8,128)(2,1)} %all-gather.7.cloned.1.call-done, bf16[2,384,2048]{2,1,0:T(8,128)(2,1)S(1)} %copy-done), kind=kOutput, calls=%fused_computation.19 | convolution fusion | flops 1614151680 | bytes 9699328 | tf_op jit(solution)/shard_map/gerd,ehd->gerh/dot_general | solution.py:28
  206.0 2.4 convert_bitcast_fusion
  208.4 6.2 %pad_maximum_fusion = bf16[4,2,2,128,2048]{4,3,0,2,1:T(8,128)(2,1)} fusion(bf16[4,1,2,128,2048]{4,3,0,2,1:T(8,128)(2,1)S(1)} %convert_bitcast_fusion, bf16[4,1,2,128,2048]{4,3,0,2,1:T(8,128)(2,1)} %convert_bitcast_fusion.1), kind=kLoop, calls=%fused_computation.1 | loop fusion | flops 4194304 | bytes 16777216 | tf_op jit(solution)/shard_map/stack | solution.py:33
  215.9 164.5 %all-reduce.3.cloned.1.call-done = bf16[4,2,2,128,2048]{4,3,0,2,1:T(8,128)(2,1)} async-done(((bf16[4,2,2,128,2048]{4,3,0,2,1:T(8,128)(2,1)}), bf16[4,2,2,128,2048]{4,3,0,2,1:T(8,128)(2,1)}) %all-reduce.3.cloned.1.call-update) | async-done | bytes 8388624
  384.8 11.0 %all-to-all-start.2 = ((bf16[1,2,128,2048]{3,1,0,2:T(2,128)(2,1)}), bf16[1,2,128,2048]{3,1,0,2:T(2,128)(2,1)S(1)}, u32[]{:S(2)}, u32[]{:S(2)}) async-start(bf16[1,2,128,2048]{3,1,0,2:T(2,128)(2,1)} %copy.37), calls=%async_computation.2 | async-start | bytes 2097152 | tf_op jit(solution)/shard_map/all_to_all | solution.py:88
  397.9 26.1 %all-to-all-done.2 = bf16[1,2,128,2048]{3,1,0,2:T(2,128)(2,1)S(1)} async-done(((bf16[1,2,128,2048]{3,1,0,2:T(2,128)(2,1)}), bf16[1,2,128,2048]{3,1,0,2:T(2,128)(2,1)S(1)}, u32[]{:S(2)}, u32[]{:S(2)}) %all-to-all-start.2) | async-done | bytes 1048608 | tf_op jit(solution)/shard_map/all_to_all | solution.py:88
  423.9 6.5 %all-to-all-start.3 = ((bf16[1,2,128,2048]{3,1,0,2:T(2,128)(2,1)}), bf16[1,2,128,2048]{3,1,0,2:T(2,128)(2,1)}, u32[]{:S(2)}, u32[]{:S(2)}) async-start(bf16[1,2,128,2048]{3,1,0,2:T(2,128)(2,1)} %copy.39), calls=%async_computation.3 | async-start | bytes 2097152 | tf_op jit(solution)/shard_map/all_to_all | solution.py:89
  430.4 6.4 %bitcast_convert_fusion.1 = bf16[2,2048,384]{2,1,0:T(8,128)(2,1)} fusion(bf16[4,2,128,2048]{3,2,0,1:T(8,128)(2,1)} %all-gather.5.cloned.1.call-done, bf16[4,2,128,384]{3,2,0,1:T(8,128)(2,1)S(1)} %copy-done.4), kind=kOutput, calls=%fused_computation.3 | convolution fusion | flops 1612185600 | bytes 8126464 | tf_op jit(solution)/shard_map/gerd,gerh->edh/dot_general | solution.py:31
  436.8 3.6 bitcast_convert_fusion
  444.1 2.4 fusion.6
  446.5 11.9 %all-to-all-done.3 = bf16[1,2,128,2048]{3,1,0,2:T(2,128)(2,1)} async-done(((bf16[1,2,128,2048]{3,1,0,2:T(2,128)(2,1)}), bf16[1,2,128,2048]{3,1,0,2:T(2,128)(2,1)}, u32[]{:S(2)}, u32[]{:S(2)}) %all-to-all-start.3) | async-done | bytes 1048608 | tf_op jit(solution)/shard_map/all_to_all | solution.py:89
  458.5 3.0 copy.74
  463.7 2.4 fusion.7
  (56 shorter events, 26.9 us)
Async XLA Ops:
  7.2 145.8 %copy-start = (bf16[2,384,2048]{2,1,0:T(8,128)(2,1)S(1)}, bf16[2,384,2048]{2,1,0:T(8,128)(2,1)}, u32[]{:S(2)}) copy-start(bf16[2,384,2048]{2,1,0:T(8,128)(2,1)} %param.16) | copy-start | bytes 9437188
  7.2 139.1 %all-gather.5.cloned.1.call-start = ((), (), s32[]{:S(2)}) async-start(), calls=%async_computation.4 | async-start | bytes 5242880 | tf_op jit(solution)/shard_map/all_gather | solution.py:78
  61.4 37.3 %copy-start.6 = (f32[16,8]{0,1:T(8,128)S(1)}, f32[16,8]{0,1:T(8,128)}, u32[]{:S(2)}) copy-start(f32[16,8]{0,1:T(8,128)} %param.12) | copy-start | bytes 1540
  61.4 37.6 %copy-start.5 = (bf16[16,2048]{1,0:T(8,128)(2,1)S(1)}, bf16[16,2048]{1,0:T(8,128)(2,1)}, u32[]{:S(2)}) copy-start(bf16[16,2048]{1,0:T(8,128)(2,1)} %param.17) | copy-start | bytes 196612
  98.7 101.2 %all-gather.7.cloned.1.call-start = ((), (), s32[]{:S(2)}) async-start(), calls=%async_computation.5 | async-start | bytes 5242880 | tf_op jit(solution)/shard_map/all_gather | solution.py:79
  141.6 238.8 %all-reduce.3.cloned.1.call-start = ((), (), s32[]{:S(2)}) async-start(), calls=%async_computation.6 | async-start | bytes 16777216
  151.8 1.1 copy-start.9
  199.8 6.2 %copy-start.2 = (bf16[2,2048,384]{2,1,0:T(8,128)(2,1)S(1)}, bf16[2,2048,384]{2,1,0:T(8,128)(2,1)}, u32[]{:S(2)}) copy-start(bf16[2,2048,384]{2,1,0:T(8,128)(2,1)} %param.15) | copy-start | bytes 9437188
  205.1 0.9 copy-start.3
  214.6 0.7 copy-start.8
  384.8 45.6 %copy-start.4 = (bf16[4,2,128,384]{3,2,0,1:T(8,128)(2,1)S(1)}, bf16[4,2,128,384]{3,2,0,1:T(8,128)(2,1)}, u32[]{:S(2)}) copy-start(bf16[4,2,128,384]{3,2,0,1:T(8,128)(2,1)} %copy-done.3) | copy-start | bytes 2359300
  384.8 39.2 %all-to-all-start.2 = ((bf16[1,2,128,2048]{3,1,0,2:T(2,128)(2,1)}), bf16[1,2,128,2048]{3,1,0,2:T(2,128)(2,1)S(1)}, u32[]{:S(2)}, u32[]{:S(2)}) async-start(bf16[1,2,128,2048]{3,1,0,2:T(2,128)(2,1)} %copy.37), calls=%async_computation.2 | async-start | bytes 2097152 | tf_op jit(solution)/shard_map/all_to_all | solution.py:88
  423.9 34.6 %all-to-all-start.3 = ((bf16[1,2,128,2048]{3,1,0,2:T(2,128)(2,1)}), bf16[1,2,128,2048]{3,1,0,2:T(2,128)(2,1)}, u32[]{:S(2)}, u32[]{:S(2)}) async-start(bf16[1,2,128,2048]{3,1,0,2:T(2,128)(2,1)} %copy.39), calls=%async_computation.3 | async-start | bytes 2097152 | tf_op jit(solution)/shard_map/all_to_all | solution.py:89
  430.4 6.4 %copy-start.7 = (bf16[4,2,128,2048]{3,2,0,1:T(8,128)(2,1)S(1)}, bf16[4,2,128,2048]{3,2,0,1:T(8,128)(2,1)}, u32[]{:S(2)}) copy-start(bf16[4,2,128,2048]{3,2,0,1:T(8,128)(2,1)} %all-gather.7.cloned.1.call-done) | copy-start | bytes 12582916
  430.4 6.4 %copy-start.10 = (f32[2,4,128,384]{3,2,1,0:T(8,128)S(1)}, f32[2,4,128,384]{3,2,1,0:T(8,128)}, u32[]{:S(2)}) copy-start(f32[2,4,128,384]{3,2,1,0:T(8,128)} %copy-done.9) | copy-start | bytes 4718596
  442.4 24.6 %copy-start.1 = (bf16[2,384,2048]{2,1,0:T(8,128)(2,1)S(1)}, bf16[2,384,2048]{2,1,0:T(8,128)(2,1)}, u32[]{:S(2)}) copy-start(bf16[2,384,2048]{2,1,0:T(8,128)(2,1)} %param.16) | copy-start | bytes 9437188
Sparse Core Ops, SparseCore 0:
  98.8 47.4 all-gather.4
  148.7 51.0 all-gather.6
  214.7 165.5 all-reduce.2
where the time goes:
time: 474 us; the launch traced here: 473 us
  waiting for transfers between devices  250 us (53%)
  blocking collectives  114 us (24%)
  matrix products  38.7 us (8%)
  local copies, waits for them, and re-layouts  31 us (7%)
  starting transfers between devices  17.7 us (4%)
  between operations  14 us (3%)
  other arithmetic  8.05 us (2%)
    unnamed x4, waiting for transfers between devices  165 us
    all_gather x1, blocking collectives, prefix(): gathered = lax.all_gather(part, axis)  44.3 us
    all_gather x1, waiting for transfers between devices, local(): lax.all_gather(g_recv, 'dp', axis=0, tiled=True)  42.5 us
    all_to_all x1, blocking collectives, local(): lax.all_to_all(x_buf, 'expert', split_axis=0, concat_axis=2, tiled=True)  35.9 us
    all_to_all x1, blocking collectives, local(): lax.all_to_all(g_buf, 'expert', split_axis=0, concat_axis=2, tiled=True)  34.2 us
    all_to_all x1, waiting for transfers between devices, local(): lax.all_to_all(out_rows, 'expert', split_axis=2, concat_axis=0, tiled=True)  26.1 us
    all_to_all x1, waiting for transfers between devices, local(): lax.all_to_all(in_rows, 'expert', split_axis=2, concat_axis=0, tiled=True)  11.9 us
    all_to_all x1, starting transfers between devices, local(): lax.all_to_all(out_rows, 'expert', split_axis=2, concat_axis=0, tiled=True)  11 us
  transfers between devices with their start and end apart: 5, of which 5 were waited for; matrix products, arithmetic and copies ran while one was open for 8% of the time, Pallas kernels for 0%

commit v1 on v0

v1 whole, which is shorter than its diff:
```python
import jax
import jax.numpy as jnp
from jax import lax
from jax.sharding import PartitionSpec as P


FLAG_COLS = 128


def silu_terms(pre_act):
    sig_val = jax.nn.sigmoid(pre_act)
    return (pre_act * sig_val, sig_val * (1.0 + pre_act * (1.0 - sig_val)))


def expert_math(rows_x, rows_g, weight_in, weight_out):
    pre_act = jnp.einsum("gerd,edh->gerh", rows_x, weight_in, preferred_element_type=jnp.float32)
    act_full, slope_val = silu_terms(pre_act)
    act_low = act_full.astype(jnp.bfloat16)
    out_part = jnp.einsum("gerh,ehd->gerd", act_low, weight_out, preferred_element_type=jnp.float32)
    back_act = jnp.einsum("gerd,ehd->gerh", rows_g, weight_out, preferred_element_type=jnp.float32)
    pre_grad = (back_act * slope_val).astype(jnp.bfloat16)
    in_part = jnp.einsum("gerh,edh->gerd", pre_grad, weight_in, preferred_element_type=jnp.float32)
    grad_in = jnp.einsum("gerd,gerh->edh", rows_x, pre_grad, preferred_element_type=jnp.float32)
    grad_out = jnp.einsum("gerh,gerd->ehd", act_low, rows_g, preferred_element_type=jnp.float32)
    stacked = jnp.stack([out_part, in_part], axis=1)
    return (stacked.astype(jnp.bfloat16), grad_in, grad_out)


def local(tokens, expert_ids, gate_weights, hot_experts, capacity, w_in, w_out, grad_y):
    highest = lax.Precision.HIGHEST
    expert_devs = lax.axis_size("expert")
    tok_rows, top_k = expert_ids.shape
    local_experts = w_in.shape[0]
    expert_total = local_experts * expert_devs
    slot_count = max(2, 3 * tok_rows * top_k // (2 * expert_total))
    feature_dim = tokens.shape[1]
    labels = jnp.arange(expert_total, dtype=jnp.int32)
    name_hit = (expert_ids[:, :, None] == labels).astype(jnp.int32)
    per_token = jnp.sum(name_hit, axis=1)
    within_dev = jnp.cumsum(per_token, axis=0) - per_token
    slot_hit = (within_dev[:, :, None] == jnp.arange(slot_count, dtype=jnp.int32)).astype(
        jnp.float32
    )
    send_picks = name_hit.astype(jnp.float32)[:, :, :, None] * slot_hit[:, None, :, :]
    rows_sel = jnp.sum(send_picks, axis=1)
    gate_sel = jnp.einsum("tkes,tk->tes", send_picks, gate_weights, precision=highest)
    grad_f32 = grad_y.astype(jnp.float32)
    x_buf = jnp.einsum(
        "tes,td->esd", rows_sel.astype(jnp.bfloat16), tokens, preferred_element_type=jnp.float32
    ).astype(jnp.bfloat16)
    g_buf = jnp.einsum("tes,td->esd", gate_sel, grad_f32, precision=highest).astype(jnp.bfloat16)
    flag = jnp.sum(gate_sel, axis=0)
    flag_cols = (jnp.arange(FLAG_COLS) == 0).astype(jnp.float32)
    flag_buf = (flag[:, :, None] * flag_cols).astype(jnp.bfloat16)
    send = jnp.concatenate([x_buf, g_buf, flag_buf], axis=-1)
    send = send.reshape(expert_devs, local_experts, slot_count, 2 * feature_dim + FLAG_COLS)
    recv = lax.all_to_all(send, "expert", split_axis=0, concat_axis=2, tiled=True)[0]
    valid = (recv[:, :, 2 * feature_dim] > 0).astype(jnp.int32)
    rank_of = jnp.cumsum(valid, axis=1) - valid
    mine = lax.axis_index("expert") * local_experts + jnp.arange(local_experts, dtype=jnp.int32)
    is_hot = jnp.any(mine[:, None] == hot_experts[None, :], axis=1)
    keep = (valid > 0) & (is_hot[:, None] | (rank_of < capacity[mine][:, None]))
    rows = jnp.where(keep[:, :, None], recv[:, :, : 2 * feature_dim], jnp.zeros((), jnp.bfloat16))
    rows_all = lax.all_gather(rows, "dp", axis=0, tiled=False)
    xg_all = rows_all[..., :feature_dim]
    gg_all = rows_all[..., feature_dim:]
    partial_terms, grad_wi, grad_wo = expert_math(xg_all, gg_all, w_in, w_out)
    parts = lax.all_to_all(partial_terms, "dp", split_axis=0, concat_axis=0, tiled=True)
    summed = jnp.sum(parts.astype(jnp.float32), axis=0).astype(jnp.bfloat16)
    summed = summed.reshape(2, local_experts, expert_devs, slot_count, feature_dim)
    back = lax.all_to_all(summed, "expert", split_axis=2, concat_axis=2, tiled=True)
    back = jnp.transpose(back, (0, 2, 1, 3, 4)).reshape(2, expert_total, slot_count, feature_dim)
    out_f32 = back[0].astype(jnp.float32)
    in_f32 = back[1].astype(jnp.float32)
    mixed = jnp.einsum("tes,esd->td", gate_sel, out_f32, precision=highest)
    token_grad = jnp.einsum("tes,esd->td", rows_sel, in_f32, precision=highest)
    dot_vals = jnp.einsum("td,esd->tes", grad_f32, out_f32, precision=highest)
    gate_grad = jnp.einsum("tkes,tes->tk", send_picks, dot_vals, precision=highest)
    return (
        mixed.astype(jnp.bfloat16),
        token_grad.astype(jnp.bfloat16),
        gate_grad,
        grad_wi.astype(jnp.bfloat16),
        grad_wo.astype(jnp.bfloat16),
    )


def solution(mesh):
    in_specs = (
        P(("dp", "expert"), None),
        P(("dp", "expert"), None),
        P(("dp", "expert"), None),
        P(),
        P(),
        P("expert", None, "dp"),
        P("expert", "dp", None),
        P(("dp", "expert"), None),
    )
    out_specs = (
        P(("dp", "expert"), None),
        P(("dp", "expert"), None),
        P(("dp", "expert"), None),
        P("expert", None, "dp"),
        P("expert", "dp", None),
    )
    return jax.shard_map(local, mesh=mesh, in_specs=in_specs, out_specs=out_specs, check_vma=False)
```

time: 474 us -> 420 us (0.89)
  waiting for transfers between devices: 250 us -> 172 us
  local copies, waits for them, and re-layouts: 31 us -> 49.3 us
  other arithmetic: 8.05 us -> 23.7 us
  blocking collectives: 114 us -> 100 us
  starting transfers between devices: 17.7 us -> 25.5 us
  matrix products: 38.7 us -> 33.8 us
    unnamed x4 -> x1, waiting for transfers between devices: 165 us -> 0.02 us
    all_to_all x2, waiting for transfers between devices: 38 us -> 88.8 us  [the longest x1 49.1 us: local(): lax.all_to_all(send, 'expert', split_axis=0, concat_axis=2, tiled=True)[0]]
    all_gather x1 -> x0, blocking collectives: 44.3 us -> none  [prefix(): gathered = lax.all_gather(part, axis)]
    all_gather x2 -> x1, waiting for transfers between devices: 47 us -> 83.2 us  [local(): rows_all = lax.all_gather(rows, 'dp', axis=0, tiled=False)]
    all_to_all x2 -> x1, blocking collectives: 70.1 us -> 100 us  [local(): lax.all_to_all(partial_terms, 'dp', split_axis=0, concat_axis=0, tiled=True)]
    slice x0 -> x6, local copies, waits for them, and re-layouts: none -> 16.3 us  [the longest x2 5.78 us: local(): in_f32 = back[1].astype(jnp.float32)]
    another operation x0 -> x1, local copies, waits for them, and re-layouts: none -> 8.27 us  [expert_math(): stacked = jnp.stack([out_part, in_part], axis=1)]
    all_to_all x2, starting transfers between devices: 17.4 us -> 25.5 us  [the longest x1 13.4 us: local(): lax.all_to_all(send, 'expert', split_axis=0, concat_axis=2, tiled=True)[0]]
  transfers between devices with their start and end apart: 5 -> 3, of which waited for: 5 -> 3; matrix products, arithmetic and copies ran while one was open for 8% -> 3% of each run, Pallas kernels for 0% -> 0%
where the time goes in v1:
time: 420 us; the launch traced here: 419 us
  waiting for transfers between devices  172 us (41%)
  blocking collectives  100 us (24%)
  local copies, waits for them, and re-layouts  49.3 us (12%)
  matrix products  33.8 us (8%)
  starting transfers between devices  25.5 us (6%)
  other arithmetic  23.7 us (6%)
  between operations  14.3 us (3%)
    all_to_all x1, blocking collectives, local(): lax.all_to_all(partial_terms, 'dp', split_axis=0, concat_axis=0, tiled=True)  100 us
    all_gather x1, waiting for transfers between devices, local(): rows_all = lax.all_gather(rows, 'dp', axis=0, tiled=False)  83.2 us
    all_to_all x1, waiting for transfers between devices, local(): lax.all_to_all(send, 'expert', split_axis=0, concat_axis=2, tiled=True)[0]  49.1 us
    all_to_all x1, waiting for transfers between devices, local(): lax.all_to_all(summed, 'expert', split_axis=2, concat_axis=2, tiled=True)  39.6 us
    all_to_all x1, starting transfers between devices, local(): lax.all_to_all(send, 'expert', split_axis=0, concat_axis=2, tiled=True)[0]  13.4 us
    all_to_all x1, starting transfers between devices, local(): lax.all_to_all(summed, 'expert', split_axis=2, concat_axis=2, tiled=True)  12.1 us
    reshape x2, local copies, waits for them, and re-layouts, local(): send.reshape(expert_devs, local_experts, slot_count, 2 * feature_dim + FL...  8.57 us
  transfers between devices with their start and end apart: 3, of which 3 were waited for; matrix products, arithmetic and copies ran while one was open for 3% of the time, Pallas kernels for 0%

profile of v1, /device:TPU:1, one launch (start us, length us, event | category | flops | bytes accessed | tf_op | source)
XLA Modules:
  0.0 418.8 jit_solution(1233907917648621226)
XLA Ops:
  14.3 4.1 reshape.82
  18.4 4.4 %copy.40 = bf16[64,2,2,4224]{3,1,2,0:T(2,128)(2,1)} copy(bf16[64,2,2,4224]{3,1,0,2:T(2,128)(2,1)} %reshape.82) | data formatting | bytes 4325376 | tf_op jit(solution)/shard_map/reshape | solution.py:56
  22.8 13.4 %all-to-all-start = ((bf16[64,2,2,4224]{3,1,2,0:T(2,128)(2,1)}), bf16[64,2,2,4224]{3,1,2,0:T(2,128)(2,1)}, u32[]{:S(2)}, u32[]{:S(2)}) async-start(bf16[64,2,2,4224]{3,1,2,0:T(2,128)(2,1)} %copy.40), calls=%async_computation | async-start | bytes 4325376 | tf_op jit(solution)/shard_map/all_to_all | solution.py:57
  38.2 49.1 %all-to-all-done = bf16[64,2,2,4224]{3,1,2,0:T(2,128)(2,1)} async-done(((bf16[64,2,2,4224]{3,1,2,0:T(2,128)(2,1)}), bf16[64,2,2,4224]{3,1,2,0:T(2,128)(2,1)}, u32[]{:S(2)}, u32[]{:S(2)}) %all-to-all-start) | async-done | bytes 2162720 | tf_op jit(solution)/shard_map/all_to_all | solution.py:57
  88.2 4.9 %slice.29 = bf16[2,128,4096]{2,0,1:T(2,128)(2,1)} slice(bf16[2,128,4224]{2,0,1:T(2,128)(2,1)} %bitcast.6), slice={[0:2], [0:128], [0:4096]} | slice | bytes 4194304 | tf_op jit(solution)/shard_map/slice | solution.py:63
  94.2 5.3 %copy_select_fusion = bf16[2,128,4096]{2,1,0:T(8,128)(2,1)} fusion(bf16[2,128,4096]{2,0,1:T(2,128)(2,1)} %slice.29, pred[2,128]{1,0:T(4,128)(4,1)S(1)} %fusion.29), kind=kLoop, calls=%fused_computation.23 | loop fusion | flops 1048576 | bytes 4194560 | tf_op jit(solution)/shard_map/jit(_where)/select_n | solution.py:63
  99.6 83.2 %all-gather.3.cloned.1.call-done = bf16[8,128,4096]{2,1,0:T(8,128)(2,1)} async-done(((bf16[2,128,4096]{2,1,0:T(8,128)(2,1)}), bf16[8,128,4096]{2,1,0:T(8,128)(2,1)}) %all-gather.3.cloned.1.call-update) | async-done | bytes 8388624 | tf_op jit(solution)/shard_map/all_gather | solution.py:64
  182.8 4.0 fusion.47
  189.5 4.3 %convert_bitcast_fusion.1 = bf16[4,1,2,128,2048]{4,3,0,2,1:T(8,128)(2,1)} fusion(bf16[2,384,2048]{2,1,0:T(8,128)(2,1)S(1)} %copy-done, f32[2,4,128,384]{3,2,1,0:T(8,128)S(1)} %fusion.4), kind=kOutput, calls=%fused_computation.5 | convolution fusion | flops 1614675968 | bytes 8912896 | tf_op jit(solution)/shard_map/gerh,ehd->gerd/dot_general | solution.py:19
  193.9 2.5 fusion.12
  197.3 4.3 %convert_bitcast_fusion = bf16[4,1,2,128,2048]{4,3,0,2,1:T(8,128)(2,1)} fusion(bf16[4,2,128,384]{3,2,0,1:T(8,128)(2,1)S(1)} %fusion.12, bf16[2,2048,384]{2,1,0:T(8,128)(2,1)S(1)} %copy-done.6), kind=kOutput, calls=%fused_computation.4 | convolution fusion | flops 1612709888 | bytes 8126464 | tf_op jit(solution)/shard_map/gerh,edh->gerd/dot_general | solution.py:22
  201.6 7.5 %pad_maximum_fusion = bf16[4,2,2,128,2048]{4,3,0,2,1:T(8,128)(2,1)} fusion(bf16[4,1,2,128,2048]{4,3,0,2,1:T(8,128)(2,1)} %convert_bitcast_fusion, bf16[4,1,2,128,2048]{4,3,0,2,1:T(8,128)(2,1)} %convert_bitcast_fusion.1), kind=kLoop, calls=%fused_computation.1 | loop fusion | flops 4194304 | bytes 16777216 | tf_op jit(solution)/shard_map/stack | solution.py:25
  209.1 8.3 %copy.44 = bf16[4,2,2,128,2048]{4,3,2,1,0:T(8,128)(2,1)} copy(bf16[4,2,2,128,2048]{4,3,0,2,1:T(8,128)(2,1)} %pad_maximum_fusion) | data formatting | bytes 16777216 | tf_op jit(solution)/shard_map/stack | solution.py:25
  217.4 100.2 %all_to_all.25 = bf16[4,2,2,128,2048]{4,3,2,1,0:T(8,128)(2,1)} all-to-all(bf16[4,2,2,128,2048]{4,3,2,1,0:T(8,128)(2,1)} %copy.44), channel_id=1, replica_groups=mesh['dp'=4,'expert'=64] {'dp'}, dimensions={0} | all-to-all | bytes 16777216 | tf_op jit(solution)/shard_map/all_to_all | solution.py:68
  317.6 7.2 %reduce_sum.42 = bf16[2,2,128,2048]{3,2,1,0:T(8,128)(2,1)} reduce(bf16[4,2,2,128,2048]{4,3,2,1,0:T(8,128)(2,1)} %all_to_all.25, bf16[]{:T(256)} %constant.10.clone.1), dimensions={0}, to_apply=%region_6.7 | reduce | flops 3145728 | bytes 10485762 | tf_op jit(solution)/shard_map/reduce_sum | solution.py:69
  324.8 3.7 copy.46
  328.6 4.1 copy.47
  332.7 12.1 %all-to-all-start.2 = ((bf16[2,2,64,2,2048]{4,1,3,0,2:T(2,128)(2,1)}), bf16[2,2,64,2,2048]{4,1,3,0,2:T(2,128)(2,1)S(1)}, u32[]{:S(2)}, u32[]{:S(2)}) async-start(bf16[2,2,64,2,2048]{4,1,3,0,2:T(2,128)(2,1)} %copy.47), calls=%async_computation.2 | async-start | bytes 4194304 | tf_op jit(solution)/shard_map/all_to_all | solution.py:71
  344.8 6.4 %bitcast_convert_fusion.1 = bf16[2,2048,384]{2,1,0:T(8,128)(2,1)} fusion(bf16[4,2,128,384]{3,2,0,1:T(8,128)(2,1)S(1)} %copy-done.8, bf16[4,2,128,2048]{3,2,1,0:T(8,128)(2,1)} %copy-done.5), kind=kOutput, calls=%fused_computation.3 | convolution fusion | flops 1612185600 | bytes 8126464 | tf_op jit(solution)/shard_map/gerd,gerh->edh/dot_general | solution.py:23
  351.2 3.6 bitcast_convert_fusion
  354.8 39.6 %all-to-all-done.2 = bf16[2,2,64,2,2048]{4,1,3,0,2:T(2,128)(2,1)S(1)} async-done(((bf16[2,2,64,2,2048]{4,1,3,0,2:T(2,128)(2,1)}), bf16[2,2,64,2,2048]{4,1,3,0,2:T(2,128)(2,1)S(1)}, u32[]{:S(2)}, u32[]{:S(2)}) %all-to-all-start.2) | async-done | bytes 2097184 | tf_op jit(solution)/shard_map/all_to_all | solution.py:71
  394.5 2.8 fusion.48
  401.0 2.4 fusion.10
  403.4 3.0 copy.49
  (69 shorter events, 23.7 us)
Async XLA Ops:
  7.2 182.4 %copy-start = (bf16[2,384,2048]{2,1,0:T(8,128)(2,1)S(1)}, bf16[2,384,2048]{2,1,0:T(8,128)(2,1)}, u32[]{:S(2)}) copy-start(bf16[2,384,2048]{2,1,0:T(8,128)(2,1)} %param.14) | copy-start | bytes 9437188
  8.3 5.9 %copy-start.12 = (f32[16,128,2]{1,2,0:T(2,128)}, f32[16,128,2]{1,2,0:T(2,128)S(1)}, u32[]{:S(2)}) copy-start(f32[16,128,2]{1,2,0:T(2,128)S(1)} %compare_convert_fusion.1) | copy-start | bytes 49156
  9.2 5.1 %copy-start.10 = (f32[16,128,2]{1,2,0:T(2,128)}, f32[16,128,2]{1,2,0:T(2,128)S(1)}, u32[]{:S(2)}) copy-start(f32[16,128,2]{1,2,0:T(2,128)S(1)} %multiply_reduce_fusion) | copy-start | bytes 49156
  22.8 13.5 %copy-start.2 = (s32[128]{0:T(128)S(1)}, s32[128]{0:T(128)}, u32[]{:S(2)}) copy-start(s32[128]{0:T(128)} %param.12) | copy-start | bytes 1540
  22.8 14.7 %copy-start.14 = (s32[2]{0:T(128)S(1)}, s32[2]{0:T(128)}, u32[]{:S(2)}) copy-start(s32[2]{0:T(128)} %param.11) | copy-start | bytes 28
  22.8 64.5 %all-to-all-start = ((bf16[64,2,2,4224]{3,1,2,0:T(2,128)(2,1)}), bf16[64,2,2,4224]{3,1,2,0:T(2,128)(2,1)}, u32[]{:S(2)}, u32[]{:S(2)}) async-start(bf16[64,2,2,4224]{3,1,2,0:T(2,128)(2,1)} %copy.40), calls=%async_computation | async-start | bytes 4325376 | tf_op jit(solution)/shard_map/all_to_all | solution.py:57
  36.3 146.5 %all-gather.3.cloned.1.call-start = ((), (), s32[]{:S(2)}) async-start(), calls=%async_computation.3 | async-start | bytes 10485760 | tf_op jit(solution)/shard_map/all_gather | solution.py:64
  182.8 4.4 %copy-start.6 = (bf16[2,2048,384]{2,1,0:T(8,128)(2,1)S(1)}, bf16[2,2048,384]{2,1,0:T(8,128)(2,1)}, u32[]{:S(2)}) copy-start(bf16[2,2048,384]{2,1,0:T(8,128)(2,1)} %param.13) | copy-start | bytes 9437188
  186.8 2.7 copy-start.5
  186.8 7.0 %copy-start.3 = (bf16[4,2,128,2048]{3,2,1,0:T(8,128)(2,1)}, bf16[4,2,128,2048]{3,2,1,0:T(8,128)(2,1)S(1)}, u32[]{:S(2)}) copy-start(bf16[4,2,128,2048]{3,2,1,0:T(8,128)(2,1)S(1)} %get-tuple-element.5) | copy-start | bytes 12582916
  189.5 4.4 %copy-start.15 = (f32[2,4,128,384]{3,2,1,0:T(8,128)}, f32[2,4,128,384]{3,2,1,0:T(8,128)S(1)}, u32[]{:S(2)}) copy-start(f32[2,4,128,384]{3,2,1,0:T(8,128)S(1)} %fusion.4) | copy-start | bytes 4718596
  196.4 0.9 copy-start.7
  332.7 12.1 %copy-start.8 = (bf16[4,2,128,384]{3,2,0,1:T(8,128)(2,1)S(1)}, bf16[4,2,128,384]{3,2,0,1:T(8,128)(2,1)}, u32[]{:S(2)}) copy-start(bf16[4,2,128,384]{3,2,0,1:T(8,128)(2,1)} %copy-done.7) | copy-start | bytes 2359300
  332.7 61.8 %all-to-all-start.2 = ((bf16[2,2,64,2,2048]{4,1,3,0,2:T(2,128)(2,1)}), bf16[2,2,64,2,2048]{4,1,3,0,2:T(2,128)(2,1)S(1)}, u32[]{:S(2)}, u32[]{:S(2)}) async-start(bf16[2,2,64,2,2048]{4,1,3,0,2:T(2,128)(2,1)} %copy.47), calls=%async_computation.2 | async-start | bytes 4194304 | tf_op jit(solution)/shard_map/all_to_all | solution.py:71
  344.8 6.4 %copy-start.4 = (bf16[4,2,128,2048]{3,2,1,0:T(8,128)(2,1)S(1)}, bf16[4,2,128,2048]{3,2,1,0:T(8,128)(2,1)}, u32[]{:S(2)}) copy-start(bf16[4,2,128,2048]{3,2,1,0:T(8,128)(2,1)} %copy-done.3) | copy-start | bytes 12582916
  344.8 6.4 %copy-start.16 = (f32[2,4,128,384]{3,2,1,0:T(8,128)S(1)}, f32[2,4,128,384]{3,2,1,0:T(8,128)}, u32[]{:S(2)}) copy-start(f32[2,4,128,384]{3,2,1,0:T(8,128)} %copy-done.15) | copy-start | bytes 4718596
  397.3 2.0 copy-start.9
  399.3 9.4 %copy-start.11 = (f32[16,128,2]{1,2,0:T(2,128)S(1)}, f32[16,128,2]{1,2,0:T(2,128)}, u32[]{:S(2)}) copy-start(f32[16,128,2]{1,2,0:T(2,128)} %copy-done.10) | copy-start | bytes 49156
  399.3 12.7 %copy-start.1 = (bf16[2,384,2048]{2,1,0:T(8,128)(2,1)S(1)}, bf16[2,384,2048]{2,1,0:T(8,128)(2,1)}, u32[]{:S(2)}) copy-start(bf16[2,384,2048]{2,1,0:T(8,128)(2,1)} %param.14) | copy-start | bytes 9437188
  401.0 10.0 %copy-start.13 = (f32[16,128,2]{1,2,0:T(2,128)S(1)}, f32[16,128,2]{1,2,0:T(2,128)}, u32[]{:S(2)}) copy-start(f32[16,128,2]{1,2,0:T(2,128)} %copy-done.12) | copy-start | bytes 49156
Sparse Core Ops, SparseCore 0:
  99.7 83.0 all-gather.2

commit v2 on v1

--- a/solution.py
+++ b/solution.py
@@ -54,22 +54,29 @@
     flag_buf = (flag[:, :, None] * flag_cols).astype(jnp.bfloat16)
     send = jnp.concatenate([x_buf, g_buf, flag_buf], axis=-1)
     send = send.reshape(expert_devs, local_experts, slot_count, 2 * feature_dim + FLAG_COLS)
-    recv = lax.all_to_all(send, "expert", split_axis=0, concat_axis=2, tiled=True)[0]
-    valid = (recv[:, :, 2 * feature_dim] > 0).astype(jnp.int32)
-    rank_of = jnp.cumsum(valid, axis=1) - valid
     mine = lax.axis_index("expert") * local_experts + jnp.arange(local_experts, dtype=jnp.int32)
     is_hot = jnp.any(mine[:, None] == hot_experts[None, :], axis=1)
-    keep = (valid > 0) & (is_hot[:, None] | (rank_of < capacity[mine][:, None]))
-    rows = jnp.where(keep[:, :, None], recv[:, :, : 2 * feature_dim], jnp.zeros((), jnp.bfloat16))
-    rows_all = lax.all_gather(rows, "dp", axis=0, tiled=False)
-    xg_all = rows_all[..., :feature_dim]
-    gg_all = rows_all[..., feature_dim:]
-    partial_terms, grad_wi, grad_wo = expert_math(xg_all, gg_all, w_in, w_out)
-    parts = lax.all_to_all(partial_terms, "dp", split_axis=0, concat_axis=0, tiled=True)
-    summed = jnp.sum(parts.astype(jnp.float32), axis=0).astype(jnp.bfloat16)
-    summed = summed.reshape(2, local_experts, expert_devs, slot_count, feature_dim)
-    back = lax.all_to_all(summed, "expert", split_axis=2, concat_axis=2, tiled=True)
-    back = jnp.transpose(back, (0, 2, 1, 3, 4)).reshape(2, expert_total, slot_count, feature_dim)
+    cap_mine = capacity[mine]
+    backs, grads_wi, grads_wo = [], [], []
+    for own in range(local_experts):
+        recv = lax.all_to_all(send[:, own], "expert", split_axis=0, concat_axis=1, tiled=True)[0]
+        valid = (recv[:, 2 * feature_dim] > 0).astype(jnp.int32)
+        rank_of = jnp.cumsum(valid) - valid
+        keep = (valid > 0) & (is_hot[own] | (rank_of < cap_mine[own]))
+        rows = jnp.where(keep[:, None], recv[:, : 2 * feature_dim], jnp.zeros((), jnp.bfloat16))
+        rows_all = lax.all_gather(rows, "dp", axis=0, tiled=False)[:, None]
+        partial_terms, grad_wi, grad_wo = expert_math(
+            rows_all[..., :feature_dim], rows_all[..., feature_dim:], w_in[own][None], w_out[own][None]
+        )
+        flat = partial_terms.reshape(-1, feature_dim)
+        summed = lax.psum_scatter(flat, "dp", scatter_dimension=0, tiled=True)
+        summed = summed.reshape(2, expert_devs, slot_count, feature_dim)
+        backs.append(lax.all_to_all(summed, "expert", split_axis=1, concat_axis=1, tiled=True))
+        grads_wi.append(grad_wi[0])
+        grads_wo.append(grad_wo[0])
+    back = jnp.stack(backs, axis=2).reshape(2, expert_total, slot_count, feature_dim)
+    grad_wi = jnp.stack(grads_wi)
+    grad_wo = jnp.stack(grads_wo)
     out_f32 = back[0].astype(jnp.float32)
     in_f32 = back[1].astype(jnp.float32)
     mixed = jnp.einsum("tes,esd->td", gate_sel, out_f32, precision=highest)

time: 420 us -> 330 us (0.79)
  blocking collectives: 100 us -> 34.9 us
  local copies, waits for them, and re-layouts: 49.3 us -> 35.8 us
  other arithmetic: 23.7 us -> 12.5 us
  starting transfers between devices: 25.5 us -> 35 us
  waiting for transfers between devices: 172 us -> 167 us
    reduce_scatter x0 -> x2, waiting for transfers between devices: none -> 77.2 us  [local(): summed = lax.psum_scatter(flat, 'dp', scatter_dimension=0, tiled=True)]
    all_to_all x1, blocking collectives: 100 us -> 34.9 us  [local(): lax.all_to_all(send[:, own], 'expert', split_axis=0, concat_axis=1, tiled...]
    all_to_all x2 -> x3, waiting for transfers between devices: 88.8 us -> 41.2 us  [the longest x1 26.7 us: local(): lax.all_to_all(send[:, own], 'expert', split_axis=0, concat_axis=1, tiled...]
    all_gather x1 -> x2, waiting for transfers between devices: 83.2 us -> 48.9 us  [local(): rows_all = lax.all_gather(rows, 'dp', axis=0, tiled=False)[:, None]]
    all_to_all x2 -> x3, starting transfers between devices: 25.5 us -> 34.7 us  [the longest x2 21.6 us: local(): lax.all_to_all(summed, 'expert', split_axis=1, concat_axis=1, tiled=True)]
    reduce_sum x1 -> x0, other arithmetic: 7.22 us -> none  [local(): summed = jnp.sum(parts.astype(jnp.float32), axis=0).astype(jnp.bfloat16)]
    another operation x1 -> x2, other arithmetic: 7.46 us -> 0.77 us  [expert_math(): stacked = jnp.stack([out_part, in_part], axis=1)]
    reshape x2 -> x1, local copies, waits for them, and re-layouts: 8.57 us -> 2.77 us  [local(): send.reshape(expert_devs, local_experts, slot_count, 2 * feature_dim + FL...]
  transfers between devices with their start and end apart: 3 -> 7, of which waited for: 3 -> 6; matrix products, arithmetic and copies ran while one was open for 3% -> 15% of each run, Pallas kernels for 0% -> 0%
where the time goes in v2:
time: 330 us
  waiting for transfers between devices  167 us (51%)
  local copies, waits for them, and re-layouts  35.8 us (11%)
  starting transfers between devices  35 us (11%)
  blocking collectives  34.9 us (11%)
  matrix products  29.6 us (9%)
  between operations  14.3 us (4%)
  other arithmetic  12.5 us (4%)
    reduce_scatter x2, waiting for transfers between devices, local(): summed = lax.psum_scatter(flat, 'dp', scatter_dimension=0, tiled=True)  77.2 us
    all_gather x2, waiting for transfers between devices, local(): rows_all = lax.all_gather(rows, 'dp', axis=0, tiled=False)[:, None]  48.9 us
    all_to_all x1, blocking collectives, local(): lax.all_to_all(send[:, own], 'expert', split_axis=0, concat_axis=1, tiled...  34.9 us
    all_to_all x1, waiting for transfers between devices, local(): lax.all_to_all(send[:, own], 'expert', split_axis=0, concat_axis=1, tiled...  26.7 us
    all_to_all x2, starting transfers between devices, local(): lax.all_to_all(summed, 'expert', split_axis=1, concat_axis=1, tiled=True)  21.6 us
    all_to_all x2, waiting for transfers between devices, local(): lax.all_to_all(summed, 'expert', split_axis=1, concat_axis=1, tiled=True)  14.5 us
    all_to_all x1, starting transfers between devices, local(): lax.all_to_all(send[:, own], 'expert', split_axis=0, concat_axis=1, tiled...  13.1 us
    reshape x4, local copies, waits for them, and re-layouts, local(): summed = summed.reshape(2, expert_devs, slot_count, feature_dim)  7.97 us
  transfers between devices with their start and end apart: 7, of which 6 were waited for; matrix products, arithmetic and copies ran while one was open for 15% of the time, Pallas kernels for 0%

profile of v2, /device:TPU:1, one launch (start us, length us, event | category | flops | bytes accessed | tf_op | source)
XLA Modules:
  0.0 329.7 jit_solution(641204137200699523)
XLA Ops:
  13.3 2.8 reshape.176
  16.1 3.9 %fusion.90 = (bf16[64,1,2,4224]{3,1,0,2:T(2,128)(2,1)}, bf16[64,1,2,4224]{3,1,0,2:T(2,128)(2,1)S(1)}) fusion(bf16[64,2,2,4224]{3,1,0,2:T(2,128)(2,1)S(1)} %reshape.176), kind=kLoop, calls=%fused_computation.122 | loop fusion | bytes 4325376 | tf_op jit(solution)/shard_map/slice | solution.py:62
  20.1 2.1 copy.55
  22.2 13.1 %all-to-all-start = ((bf16[64,2,4224]{2,1,0:T(2,128)(2,1)}), bf16[64,2,4224]{2,1,0:T(2,128)(2,1)S(1)}, u32[]{:S(2)}, u32[]{:S(2)}) async-start(bf16[64,2,4224]{2,1,0:T(2,128)(2,1)} %copy.55), calls=%async_computation | async-start | bytes 2162688 | tf_op jit(solution)/shard_map/all_to_all | solution.py:62
  37.5 26.7 %all-to-all-done = bf16[64,2,4224]{2,1,0:T(2,128)(2,1)S(1)} async-done(((bf16[64,2,4224]{2,1,0:T(2,128)(2,1)}), bf16[64,2,4224]{2,1,0:T(2,128)(2,1)S(1)}, u32[]{:S(2)}, u32[]{:S(2)}) %all-to-all-start) | async-done | bytes 1081376 | tf_op jit(solution)/shard_map/all_to_all | solution.py:62
  68.8 34.9 %all_to_all.28 = bf16[64,2,4224]{2,1,0:T(2,128)(2,1)S(1)} all-to-all(bf16[64,2,4224]{2,1,0:T(2,128)(2,1)S(1)} %copy.60), channel_id=1, replica_groups=mesh['dp'=4,'expert'=64] {'expert'}, dimensions={0} | all-to-all | bytes 2162688 | tf_op jit(solution)/shard_map/all_to_all | solution.py:62
  107.1 8.0 %all-gather.5.cloned.1.call-done = bf16[512,4096]{1,0:T(8,128)(2,1)} async-done(((bf16[128,4096]{1,0:T(8,128)(2,1)}), bf16[512,4096]{1,0:T(8,128)(2,1)}) %all-gather.5.cloned.1.call-update) | async-done | bytes 4194320 | tf_op jit(solution)/shard_map/all_gather | solution.py:67
  115.1 3.4 %fusion.39 = f32[4,1,128,384]{3,2,0,1:T(8,128)S(1)} fusion(bf16[2,2048,384]{2,1,0:T(8,128)(2,1)} %param.13, bf16[4,1,128,4096]{3,2,0,1:T(8,128)(2,1)} %bitcast.258), kind=kOutput, calls=%fused_computation.57 | convolution fusion | flops 805306368 | bytes 4456448 | tf_op jit(solution)/shard_map/gerd,edh->gerh/dot_general | solution.py:16
  118.6 3.1 fusion.54
  125.4 2.3 copy.56
  127.8 40.9 %all-gather.7.cloned.1.call-done = bf16[512,4096]{1,0:T(8,128)(2,1)} async-done(((bf16[128,4096]{1,0:T(8,128)(2,1)}), bf16[512,4096]{1,0:T(8,128)(2,1)}) %all-gather.7.cloned.1.call-update) | async-done | bytes 4194320 | tf_op jit(solution)/shard_map/all_gather | solution.py:67
  168.7 3.0 fusion.33
  171.7 3.0 fusion.57
  178.4 2.2 copy.61
  180.7 40.4 %reduce-scatter.3.cloned.1.call-done = bf16[256,2048]{1,0:T(8,128)(2,1)} async-done(((bf16[1024,2048]{1,0:T(8,128)(2,1)}), bf16[256,2048]{1,0:T(8,128)(2,1)}) %reduce-scatter.3.cloned.1.call-update) | async-done | bytes 1048592 | tf_op jit(solution)/shard_map/reduce_scatter | solution.py:72
  222.8 2.2 copy.57
  225.0 10.8 %all-to-all-start.1 = ((bf16[2,64,2,2048]{3,2,0,1:T(2,128)(2,1)}), bf16[2,64,2,2048]{3,2,0,1:T(2,128)(2,1)S(1)}, u32[]{:S(2)}, u32[]{:S(2)}) async-start(bf16[2,64,2,2048]{3,2,0,1:T(2,128)(2,1)} %copy.57), calls=%async_computation.2 | async-start | bytes 2097152 | tf_op jit(solution)/shard_map/all_to_all | solution.py:74
  235.8 36.8 %reduce-scatter.5.cloned.1.call-done = bf16[256,2048]{1,0:T(8,128)(2,1)} async-done(((bf16[1024,2048]{1,0:T(8,128)(2,1)}), bf16[256,2048]{1,0:T(8,128)(2,1)}) %reduce-scatter.5.cloned.1.call-update) | async-done | bytes 1048592 | tf_op jit(solution)/shard_map/reduce_scatter | solution.py:72
  274.4 2.3 copy.62
  276.7 10.8 %all-to-all-start.3 = ((bf16[2,64,2,2048]{3,2,0,1:T(2,128)(2,1)}), bf16[2,64,2,2048]{3,2,0,1:T(2,128)(2,1)S(1)}, u32[]{:S(2)}, u32[]{:S(2)}) async-start(bf16[2,64,2,2048]{3,2,0,1:T(2,128)(2,1)} %copy.62), calls=%async_computation.5 | async-start | bytes 2097152 | tf_op jit(solution)/shard_map/all_to_all | solution.py:74
  287.5 2.8 fusion.6
  291.6 1.9 pad_maximum_fusion.3
  297.6 2.0 pad_maximum_fusion.2
  301.2 14.5 %all-to-all-done.3 = bf16[2,64,2,2048]{3,2,0,1:T(2,128)(2,1)S(1)} async-done(((bf16[2,64,2,2048]{3,2,0,1:T(2,128)(2,1)}), bf16[2,64,2,2048]{3,2,0,1:T(2,128)(2,1)S(1)}, u32[]{:S(2)}, u32[]{:S(2)}) %all-to-all-start.3) | async-done | bytes 1048608 | tf_op jit(solution)/shard_map/all_to_all | solution.py:74
  (108 shorter events, 41.4 us)
Async XLA Ops:
  7.2 2.2 copy-start
  20.1 15.4 %copy-start.1 = (s32[128]{0:T(128)S(1)}, s32[128]{0:T(128)}, u32[]{:S(2)}) copy-start(s32[128]{0:T(128)} %param.12) | copy-start | bytes 1540
  20.1 16.6 %copy-start.15 = (s32[2]{0:T(128)S(1)}, s32[2]{0:T(128)}, u32[]{:S(2)}) copy-start(s32[2]{0:T(128)} %param.11) | copy-start | bytes 28
  22.2 42.0 %all-to-all-start = ((bf16[64,2,4224]{2,1,0:T(2,128)(2,1)}), bf16[64,2,4224]{2,1,0:T(2,128)(2,1)S(1)}, u32[]{:S(2)}, u32[]{:S(2)}) async-start(bf16[64,2,4224]{2,1,0:T(2,128)(2,1)} %copy.55), calls=%async_computation | async-start | bytes 2162688 | tf_op jit(solution)/shard_map/all_to_all | solution.py:62
  35.4 79.8 %all-gather.5.cloned.1.call-start = ((), (), s32[]{:S(2)}) async-start(), calls=%async_computation.8 | async-start | bytes 5242880 | tf_op jit(solution)/shard_map/all_gather | solution.py:67
  64.6 2.9 copy-start.2
  67.5 101.2 %all-gather.7.cloned.1.call-start = ((), (), s32[]{:S(2)}) async-start(), calls=%async_computation.9 | async-start | bytes 5242880 | tf_op jit(solution)/shard_map/all_gather | solution.py:67
  106.9 114.2 %reduce-scatter.3.cloned.1.call-start = ((), (), s32[]{:S(2)}) async-start(), calls=%async_computation.6 | async-start | bytes 5242880 | tf_op jit(solution)/shard_map/reduce_scatter | solution.py:72
  115.1 3.4 %copy-start.9 = (bf16[512,4096]{1,0:T(8,128)(2,1)S(1)}, bf16[512,4096]{1,0:T(8,128)(2,1)}, u32[]{:S(2)}) copy-start(bf16[512,4096]{1,0:T(8,128)(2,1)} %all-gather.5.cloned.1.call-done) | copy-start | bytes 12582916
  118.6 4.4 %copy-start.16 = (f32[4,1,128,384]{3,2,0,1:T(8,128)}, f32[4,1,128,384]{3,2,0,1:T(8,128)S(1)}, u32[]{:S(2)}) copy-start(f32[4,1,128,384]{3,2,0,1:T(8,128)S(1)} %fusion.39) | copy-start | bytes 2359300
  118.6 3.1 copy-start.4
  121.7 2.0 copy-start.13
  127.7 144.9 %reduce-scatter.5.cloned.1.call-start = ((), (), s32[]{:S(2)}) async-start(), calls=%async_computation.7 | async-start | bytes 5242880 | tf_op jit(solution)/shard_map/reduce_scatter | solution.py:72
  168.7 3.0 copy-start.11
  171.7 4.4 %copy-start.18 = (f32[4,1,128,384]{3,2,0,1:T(8,128)}, f32[4,1,128,384]{3,2,0,1:T(8,128)S(1)}, u32[]{:S(2)}) copy-start(f32[4,1,128,384]{3,2,0,1:T(8,128)S(1)} %fusion.33) | copy-start | bytes 2359300
  174.7 2.0 copy-start.14
  225.0 51.7 %all-to-all-start.1 = ((bf16[2,64,2,2048]{3,2,0,1:T(2,128)(2,1)}), bf16[2,64,2,2048]{3,2,0,1:T(2,128)(2,1)S(1)}, u32[]{:S(2)}, u32[]{:S(2)}) async-start(bf16[2,64,2,2048]{3,2,0,1:T(2,128)(2,1)} %copy.57), calls=%async_computation.2 | async-start | bytes 2097152 | tf_op jit(solution)/shard_map/all_to_all | solution.py:74
  274.4 13.1 %copy-start.17 = (f32[4,1,128,384]{3,2,0,1:T(8,128)S(1)}, f32[4,1,128,384]{3,2,0,1:T(8,128)}, u32[]{:S(2)}) copy-start(f32[4,1,128,384]{3,2,0,1:T(8,128)} %copy-done.16) | copy-start | bytes 2359300
  276.7 39.0 %all-to-all-start.3 = ((bf16[2,64,2,2048]{3,2,0,1:T(2,128)(2,1)}), bf16[2,64,2,2048]{3,2,0,1:T(2,128)(2,1)S(1)}, u32[]{:S(2)}, u32[]{:S(2)}) async-start(bf16[2,64,2,2048]{3,2,0,1:T(2,128)(2,1)} %copy.62), calls=%async_computation.5 | async-start | bytes 2097152 | tf_op jit(solution)/shard_map/all_to_all | solution.py:74
  287.5 2.8 copy-start.12
  287.5 3.0 copy-start.19
  291.6 2.0 copy-start.6
  291.6 3.4 %copy-start.10 = (bf16[512,4096]{1,0:T(8,128)(2,1)S(1)}, bf16[512,4096]{1,0:T(8,128)(2,1)}, u32[]{:S(2)}) copy-start(bf16[512,4096]{1,0:T(8,128)(2,1)} %all-gather.5.cloned.1.call-done) | copy-start | bytes 12582916
  301.2 15.0 %copy-start.3 = (bf16[2,64,2,2048]{3,1,2,0:T(8,128)(2,1)S(1)}, bf16[2,64,2,2048]{3,1,2,0:T(8,128)(2,1)}, u32[]{:S(2)}) copy-start(bf16[2,64,2,2048]{3,1,2,0:T(8,128)(2,1)} %copy.103) | copy-start | bytes 3145732
  (3 other events, 4.0 us)
Sparse Core Ops, SparseCore 0:
  67.6 47.5 all-gather.4
  117.5 51.0 all-gather.6
  171.2 49.8 reduce-scatter.2
  223.5 49.1 reduce-scatter.4
